TPU v7x, 128 devices: a whole 4x4x4 slice. The times are simulated.
128 devices in a mesh: tok: 8 (over z, core), wid: 16 (over y, x).
Axes of the slice: x: 4, y: 4, z: 4, core: 2. Of those that a mesh axis runs over, the one named last changes fastest.
Arguments:
- tokens: bfloat16 [8192, 3072], P('tok', 'wid'), may hold values from -6 to 6
- defect_mask: int32 [8192], P('tok'), may hold values 0 or 1
- timestep: int32 [1], replicated, may hold values from 0 to 999
- mask_embed: bfloat16 [3072], P('wid'), may hold values from -6 to 6
- mod_weight: bfloat16 [256, 3, 3072], P(None, None, 'wid'), may hold values from -0.375 to 0.375
- w_qkv: bfloat16 [3072, 3, 2048], P('tok', None, 'wid'), may hold values from -1.4614179 to 1.4614179, as said below
- w_out: bfloat16 [2048, 3072], P('wid'), may hold values from -0.125 to 0.125
Outputs:
- block_out: bfloat16 [8192, 3072], P('tok', 'wid')
Inputs may be any that keep to these rules, and one draw needn't show every extreme that they name: `w_qkv`: entries are at most 81 / sqrt(3072) in magnitude.
All inputs are finite; a program needn't handle non-finite values. No bound on the sum of `defect_mask` on one device may be relied on, other than what follows from the above.
Results may differ from a plain program's by a relative error of at most 0.011.
Values may be sent and summed in bfloat16 or wider, within the bound.
No kernel may reach another device: no remote copies, remote signals or barrier semaphores. Data moves between devices by JAX's collectives and lax.ppermute only.
A program may use at most 128 MiB of HBM per device.

v0:
```python
import math
import jax
import jax.numpy as jnp
from jax import lax
from jax.sharding import PartitionSpec as P

D = 3072
DH = 128
TEMB = 256


def finish_rows(values, row_mean, row_var, shift_row, scale_row):
    normal = (values - row_mean) * lax.rsqrt(row_var + 1e-06)
    return (normal * (1.0 + scale_row.astype(jnp.float32)) + shift_row.astype(jnp.float32)).astype(
        jnp.bfloat16
    )


def body(tokens, defect_mask, timestep, mask_embed, mod_weight, w_qkv, w_out):
    tok_rows = tokens.shape[0]
    residual_in = (
        tokens.astype(jnp.float32)
        + defect_mask.astype(jnp.float32)[:, None] * mask_embed.astype(jnp.float32)[None, :]
    ).astype(jnp.bfloat16)
    w_cols = lax.all_to_all(w_out, "wid", split_axis=1, concat_axis=0, tiled=True)
    w_full = lax.all_gather(w_qkv, "tok", axis=0, tiled=True)
    residual_full = lax.all_gather(residual_in, "wid", axis=1, tiled=True)
    half_width = TEMB // 2
    frequency = jnp.exp(-math.log(10000.0) * jnp.arange(half_width, dtype=jnp.float32) / half_width)
    angles = timestep.astype(jnp.float32)[0] * frequency
    embedding = jnp.concatenate([jnp.cos(angles), jnp.sin(angles)])
    modulation = jnp.einsum(
        "e,ecf->cf",
        jax.nn.silu(embedding),
        mod_weight.astype(jnp.float32),
        precision=lax.Precision.HIGHEST,
    ).astype(jnp.bfloat16)
    shift_scale = lax.all_gather(modulation[:2], "wid", axis=1, tiled=True)
    values = residual_full.astype(jnp.float32)
    row_mean = jnp.mean(values, axis=1, keepdims=True)
    row_var = jnp.mean(values * values, axis=1, keepdims=True) - row_mean * row_mean
    normed = finish_rows(
        values, row_mean, row_var, shift_scale[0][None, :], shift_scale[1][None, :]
    )
    qkv = jnp.einsum("td,dcf->tcf", normed, w_full, preferred_element_type=jnp.float32).astype(
        jnp.bfloat16
    )
    queries = qkv[:, 0]
    key_values = lax.all_gather(qkv[:, 1:3], "tok", axis=0, tiled=True)
    key_part = key_values[:, 0]
    value_part = key_values[:, 1]
    score_scale = DH ** (-0.5)
    scores = jnp.dot(queries, key_part.T, preferred_element_type=jnp.float32) * score_scale
    shifted = jnp.exp(scores - jnp.max(scores, axis=1, keepdims=True))
    row_sum = jnp.sum(shifted, axis=1, keepdims=True)
    numer = jnp.dot(shifted.astype(jnp.bfloat16), value_part, preferred_element_type=jnp.float32)
    attended = (numer / row_sum).astype(jnp.bfloat16)
    attended_full = lax.all_gather(attended, "wid", axis=1, tiled=True)
    projected = jnp.dot(attended_full, w_cols, preferred_element_type=jnp.float32)
    return (
        residual_in.astype(jnp.float32) + modulation[2].astype(jnp.float32)[None, :] * projected
    ).astype(jnp.bfloat16)


def solution(mesh):
    return jax.shard_map(
        body,
        mesh=mesh,
        in_specs=(
            P("tok", "wid"),
            P("tok"),
            P(),
            P("wid"),
            P(None, None, "wid"),
            P("tok", None, "wid"),
            P("wid", None),
        ),
        out_specs=P("tok", "wid"),
        check_vma=False,
    )
```

profile of v0, /device:TPU:0, one launch (start us, length us, event | category | flops | bytes accessed | tf_op | source)
XLA Modules:
  0.0 257.7 jit_solution(2055310667974810968)
XLA Ops:
  6.5 0.0 copy-start
  6.5 0.0 all-gather.6.cloned.1.call-start
  6.5 0.7 convert_element_type.47
  7.3 0.7 convert_element_type.48
  7.9 1.9 add_convert_fusion
  9.8 0.0 all-gather.6.cloned.1.call-update
  9.9 0.0 all-gather.8.cloned.1.call-start
  9.9 0.7 all-gather.8.cloned.1.call-update
  10.6 0.0 all-gather.10.cloned.1.call-start
  11.4 0.0 copy-done
  11.4 0.3 fusion.30
  11.8 23.8 %all-gather = bf16[16,192,2]{1,2,0:T(2,128)(2,1)S(1)} all-gather(bf16[1,192,2]{1,2,0:T(2,128)(2,1)S(1)} %slice_bitcast_fusion.10), channel_id=1, replica_groups=mesh['tok'=8,'wid'=16] {'wid'}, dimensions={0}, use_global_device_ids=true | all-gather | bytes 13056 | tf_op jit(solution)/shard_map/all_gather | solution.py:38
  35.6 0.1 reshape.28
  35.7 38.0 %all-gather.6.cloned.1.call-done = bf16[1024,3072]{0,1:T(8,128)(2,1)} async-done(((bf16[1024,192]{0,1:T(8,128)(2,1)}), bf16[1024,3072]{0,1:T(8,128)(2,1)}) %all-gather.6.cloned.1.call-update) | async-done | bytes 6291472 | tf_op jit(solution)/shard_map/all_gather | solution.py:27
  73.7 4.5 %convert_reduce_fusion = (f32[1024]{0:T(1024)S(1)}, f32[1024]{0:T(1024)S(1)}) fusion(bf16[1024,3072]{0,1:T(8,128)(2,1)} %all-gather.6.cloned.1.call-done), kind=kLoop, calls=%fused_computation.6 | loop fusion | flops 12580864 | bytes 6299648 | tf_op jit(solution)/shard_map/reduce_sum | solution.py:40
  78.2 22.8 %all-gather.8.cloned.1.call-done = bf16[3072,3,128]{2,0,1:T(8,128)(2,1)} async-done(((bf16[384,3,128]{2,0,1:T(8,128)(2,1)}), bf16[3072,3,128]{2,0,1:T(8,128)(2,1)}) %all-gather.8.cloned.1.call-update) | async-done | bytes 2359312 | tf_op jit(solution)/shard_map/all_gather | solution.py:26
  100.9 7.2 %fusion.13 = bf16[1024,3,128]{2,0,1:T(8,128)(2,1)S(1)} fusion(bf16[3072,3,128]{2,0,1:T(8,128)(2,1)} %all-gather.8.cloned.1.call-done, bf16[1024,3072]{0,1:T(8,128)(2,1)} %all-gather.6.cloned.1.call-done, f32[3072]{0:T(1024)S(1)} %bitcast.53, f32[3072]{0:T(1024)S(1)} %bitcast.52, f32[1024]{0:T(1024)S(1)} %get-tuple-element.8, f32[1024]{0:T(1024)S(1)} %get-tuple-element.7), kind=kOutput, calls=%fused_computation.18 | convolution fusion | flops 2435186688 | bytes 9469952 | tf_op jit(solution)/shard_map/td,dcf->tcf/dot_general | solution.py:45
  108.1 0.8 slice.37
  109.0 0.0 all-gather.10.cloned.1.call-update
  109.0 0.2 all-gather.12.cloned.1.call-start
  109.2 32.7 %all-gather.10.cloned.1.call-done = bf16[8192,2,128]{2,0,1:T(8,128)(2,1)} async-done(((bf16[1024,2,128]{2,0,1:T(8,128)(2,1)}), bf16[8192,2,128]{2,0,1:T(8,128)(2,1)}) %all-gather.10.cloned.1.call-update) | async-done | bytes 4194320 | tf_op jit(solution)/shard_map/all_gather | solution.py:49
  141.9 14.7 %multiply_reduce_fusion = (f32[1024]{0:T(1024)S(1)}, f32[1024,8192]{1,0:T(8,128)}) fusion(bf16[8192,2,128]{2,0,1:T(8,128)(2,1)} %all-gather.10.cloned.1.call-done, bf16[1024,3,128]{2,0,1:T(8,128)(2,1)S(1)} %fusion.13), kind=kOutput, calls=%fused_computation.1 | convolution fusion | flops 2164259840 | bytes 35917824 | tf_op jit(solution)/shard_map/dot_general | solution.py:53
  156.5 0.0 copy-start.2
  156.5 14.3 %fusion = f32[1024]{0:T(1024)S(1)} fusion(f32[1024,8192]{1,0:T(8,128)} %get-tuple-element.10, f32[1024]{0:T(1024)S(1)} %get-tuple-element.9), kind=kLoop, calls=%fused_computation.2 | loop fusion | flops 25164800 | bytes 33562624 | tf_op jit(solution)/shard_map/reduce_sum | solution.py:55
  170.8 0.0 copy-done.2
  170.8 0.0 copy-start.3
  170.8 0.0 copy-start.1
  170.8 14.2 %fusion.21 = bf16[1024,128]{1,0:T(8,128)(2,1)} fusion(bf16[8192,2,128]{2,0,1:T(8,128)(2,1)S(1)} %copy-done.2, f32[1024,8192]{1,0:T(8,128)} %get-tuple-element.10, f32[1024]{0:T(1024)S(1)} %get-tuple-element.9, f32[1024]{0:T(1024)S(1)} %fusion), kind=kOutput, calls=%fused_computation.23 | convolution fusion | flops 2172911616 | bytes 35921920 | tf_op jit(solution)/shard_map/dot_general | solution.py:56
  185.0 0.0 all-gather.12.cloned.1.call-update
  185.0 0.0 copy-done.3
  185.0 1.2 copy.18
  186.2 6.8 %all-to-all-start = ((bf16[128,16,192]{0,2,1:T(8,128)(2,1)}), bf16[128,16,192]{0,2,1:T(8,128)(2,1)S(1)}, u32[]{:S(2)}, u32[]{:S(2)}) async-start(bf16[128,16,192]{0,2,1:T(8,128)(2,1)} %bitcast.13), calls=%async_computation | async-start | bytes 1572864 | tf_op jit(solution)/shard_map/all_to_all | solution.py:25
  193.0 17.5 %all-to-all-done = bf16[128,16,192]{0,2,1:T(8,128)(2,1)S(1)} async-done(((bf16[128,16,192]{0,2,1:T(8,128)(2,1)}), bf16[128,16,192]{0,2,1:T(8,128)(2,1)S(1)}, u32[]{:S(2)}, u32[]{:S(2)}) %all-to-all-start) | async-done | bytes 786464 | tf_op jit(solution)/shard_map/all_to_all | solution.py:25
  210.6 36.1 %all-gather.12.cloned.1.call-done = bf16[1024,2048]{1,0:T(8,128)(2,1)} async-done(((bf16[1024,128]{1,0:T(8,128)(2,1)}), bf16[1024,2048]{1,0:T(8,128)(2,1)}) %all-gather.12.cloned.1.call-update) | async-done | bytes 4194320 | tf_op jit(solution)/shard_map/all_gather | solution.py:58
  246.7 0.0 copy-done.1
  246.7 4.5 %fusion.17 = bf16[1024,192]{0,1:T(8,128)(2,1)} fusion(bf16[1024,2048]{1,0:T(8,128)(2,1)} %all-gather.12.cloned.1.call-done, bf16[1024,192]{0,1:T(8,128)(2,1)S(1)} %copy-done.1, f32[192]{0:T(256)S(1)} %bitcast.57, bf16[128,16,192]{0,2,1:T(8,128)(2,1)S(1)} %all-to-all-done), kind=kOutput, calls=%fused_computation.21 | convolution fusion | flops 806092800 | bytes 5767936 | tf_op jit(solution)/shard_map/dot_general | solution.py:59
  (9 shorter events, 0.1 us)
Async XLA Ops:
  6.5 4.8 %copy-start = (bf16[256,3,192]{0,2,1:T(8,128)(2,1)S(1)}, bf16[256,3,192]{0,2,1:T(8,128)(2,1)}, u32[]{:S(2)}) copy-start(bf16[256,3,192]{0,2,1:T(8,128)(2,1)} %param.11) | copy-start | bytes 884740
  6.5 67.1 %all-gather.6.cloned.1.call-start = ((), (), s32[]{:S(2)}) async-start(), calls=%async_computation.1 | async-start | bytes 6684672 | tf_op jit(solution)/shard_map/all_gather | solution.py:27
  9.9 91.1 %all-gather.8.cloned.1.call-start = ((), (), s32[]{:S(2)}) async-start(), calls=%async_computation.2 | async-start | bytes 2654208 | tf_op jit(solution)/shard_map/all_gather | solution.py:26
  10.6 131.3 %all-gather.10.cloned.1.call-start = ((), (), s32[]{:S(2)}) async-start(), calls=%async_computation.3 | async-start | bytes 4718592 | tf_op jit(solution)/shard_map/all_gather | solution.py:49
  109.0 137.7 %all-gather.12.cloned.1.call-start = ((), (), s32[]{:S(2)}) async-start(), calls=%async_computation.4 | async-start | bytes 4456448 | tf_op jit(solution)/shard_map/all_gather | solution.py:58
  156.5 14.3 %copy-start.2 = (bf16[8192,2,128]{2,0,1:T(8,128)(2,1)S(1)}, bf16[8192,2,128]{2,0,1:T(8,128)(2,1)}, u32[]{:S(2)}) copy-start(bf16[8192,2,128]{2,0,1:T(8,128)(2,1)} %all-gather.10.cloned.1.call-done) | copy-start | bytes 12582916
  170.8 14.2 %copy-start.3 = (bf16[128,3072]{1,0:T(8,128)(2,1)S(1)}, bf16[128,3072]{1,0:T(8,128)(2,1)}, u32[]{:S(2)}) copy-start(bf16[128,3072]{1,0:T(8,128)(2,1)} %param.13) | copy-start | bytes 2359300
  170.8 75.8 %copy-start.1 = (bf16[1024,192]{0,1:T(8,128)(2,1)S(1)}, bf16[1024,192]{0,1:T(8,128)(2,1)}, u32[]{:S(2)}) copy-start(bf16[1024,192]{0,1:T(8,128)(2,1)} %add_convert_fusion) | copy-start | bytes 1179652
  186.2 24.4 %all-to-all-start = ((bf16[128,16,192]{0,2,1:T(8,128)(2,1)}), bf16[128,16,192]{0,2,1:T(8,128)(2,1)S(1)}, u32[]{:S(2)}, u32[]{:S(2)}) async-start(bf16[128,16,192]{0,2,1:T(8,128)(2,1)} %bitcast.13), calls=%async_computation | async-start | bytes 1572864 | tf_op jit(solution)/shard_map/all_to_all | solution.py:25
Sparse Core Ops, SparseCore 0:
  10.0 63.6 all-gather.5
  75.4 25.5 all-gather.7
  109.1 32.7 all-gather.9
  185.2 61.4 all-gather.11
where the time goes:
time: 258 us
  waiting for transfers between devices  148 us (57%)
  matrix products  40.9 us (16%)
  blocking collectives  23.8 us (9%)
  other arithmetic  22.1 us (9%)
  between operations  13.9 us (5%)
  starting transfers between devices  7.11 us (3%)
    all_gather x1, waiting for transfers between devices, body(): residual_full = lax.all_gather(residual_in, 'wid', axis=1, tiled=True)  38 us
    all_gather x1, waiting for transfers between devices, body(): attended_full = lax.all_gather(attended, 'wid', axis=1, tiled=True)  36.1 us
    all_gather x1, waiting for transfers between devices, body(): key_values = lax.all_gather(qkv[:, 1:3], 'tok', axis=0, tiled=True)  32.7 us
    all_gather x1, blocking collectives, body(): shift_scale = lax.all_gather(modulation[:2], 'wid', axis=1, tiled=True)  23.8 us
    all_gather x1, waiting for transfers between devices, body(): w_full = lax.all_gather(w_qkv, 'tok', axis=0, tiled=True)  22.8 us
    all_to_all x1, waiting for transfers between devices, body(): lax.all_to_all(w_out, 'wid', split_axis=1, concat_axis=0, tiled=True)  17.5 us
    dot_general x1, matrix products, body(): jnp.dot(queries, key_part.T, preferred_element_type=jnp.float32)  14.7 us
    reduce_sum x1, other arithmetic, body(): row_sum = jnp.sum(shifted, axis=1, keepdims=True)  14.3 us
  transfers between devices with their start and end apart: 5, of which 5 were waited for; matrix products, arithmetic and copies ran while one was open for 2% of the time, Pallas kernels for 0%

commit v1 on v0

--- a/solution.py
+++ b/solution.py
@@ -7,6 +7,22 @@
 D = 3072
 DH = 128
 TEMB = 256
+
+
+def summed_both_ways(x, axis, dim, contribution):
+    size, index, extent = (lax.axis_size(axis), lax.axis_index(axis), x.shape[dim])
+    right = [(i, (i + 1) % size) for i in range(size)]
+    downward = [(i, (i - 1) % size) for i in range(size)]
+    half = size // 2
+    from_left = from_right = x
+    total = contribution(x, index * extent)
+    for hop in range(1, half + 1):
+        from_left = lax.ppermute(from_left, axis, right)
+        if hop < size - half:
+            from_right = lax.ppermute(from_right, axis, downward)
+            total = total + contribution(from_right, (index + hop) % size * extent)
+        total = total + contribution(from_left, (index - hop) % size * extent)
+    return total
 
 
 def finish_rows(values, row_mean, row_var, shift_row, scale_row):
@@ -23,7 +39,6 @@
         + defect_mask.astype(jnp.float32)[:, None] * mask_embed.astype(jnp.float32)[None, :]
     ).astype(jnp.bfloat16)
     w_cols = lax.all_to_all(w_out, "wid", split_axis=1, concat_axis=0, tiled=True)
-    w_full = lax.all_gather(w_qkv, "tok", axis=0, tiled=True)
     residual_full = lax.all_gather(residual_in, "wid", axis=1, tiled=True)
     half_width = TEMB // 2
     frequency = jnp.exp(-math.log(10000.0) * jnp.arange(half_width, dtype=jnp.float32) / half_width)
@@ -42,9 +57,17 @@
     normed = finish_rows(
         values, row_mean, row_var, shift_scale[0][None, :], shift_scale[1][None, :]
     )
-    qkv = jnp.einsum("td,dcf->tcf", normed, w_full, preferred_element_type=jnp.float32).astype(
-        jnp.bfloat16
-    )
+    qkv = summed_both_ways(
+        w_qkv,
+        "tok",
+        0,
+        lambda shard, at: jnp.einsum(
+            "td,dcf->tcf",
+            lax.dynamic_slice_in_dim(normed, at, shard.shape[0], axis=1),
+            shard,
+            preferred_element_type=jnp.float32,
+        ),
+    ).astype(jnp.bfloat16)
     queries = qkv[:, 0]
     key_values = lax.all_gather(qkv[:, 1:3], "tok", axis=0, tiled=True)
     key_part = key_values[:, 0]

time: 258 us -> 246 us (0.953)
  waiting for transfers between devices: 148 us -> 115 us
  starting transfers between devices: 7.11 us -> 16.6 us
  local copies, waits for them, and re-layouts: 2.14 us -> 10.8 us
  other arithmetic: 22.1 us -> 26.3 us
    all_gather x1 -> x0, waiting for transfers between devices: 22.8 us -> none  [body(): w_full = lax.all_gather(w_qkv, 'tok', axis=0, tiled=True)]
    all_gather x1, waiting for transfers between devices: 38 us -> 20.4 us  [body(): residual_full = lax.all_gather(residual_in, 'wid', axis=1, tiled=True)]
    ppermute x0 -> x7, starting transfers between devices: none -> 9.54 us  [the longest x3 9.52 us: summed_both_ways(): from_right = lax.ppermute(from_right, axis, downward)]
    all_gather x0 -> x1, local copies, waits for them, and re-layouts: none -> 8.63 us  [body(): residual_full = lax.all_gather(residual_in, 'wid', axis=1, tiled=True)]
    ppermute x0 -> x7, waiting for transfers between devices: none -> 8.59 us  [the longest x4 8.58 us: summed_both_ways(): from_left = lax.ppermute(from_left, axis, right)]
    convert_element_type x0 -> x1, other arithmetic: none -> 3.81 us  [finish_rows(): (normal * (1.0 + scale_row.astype(jnp.float32)) + shift_row.astype(jnp.fl...]
    dot_general x1 -> x8, matrix products: 7.21 us -> 5.47 us  [body(): jnp.einsum('td,dcf->tcf', lax.dynamic_slice_in_dim(normed, at, shard.shap...]
  transfers between devices with their start and end apart: 5 -> 11, of which waited for: 5 -> 6; matrix products, arithmetic and copies ran while one was open for 2% -> 10% of each run, Pallas kernels for 0% -> 0%
where the time goes in v1:
time: 246 us; the launch traced here: 245 us
  waiting for transfers between devices  115 us (47%)
  matrix products  39.2 us (16%)
  other arithmetic  26.3 us (11%)
  blocking collectives  23.7 us (10%)
  starting transfers between devices  16.6 us (7%)
  between operations  14.2 us (6%)
  local copies, waits for them, and re-layouts  10.8 us (4%)
    all_gather x1, waiting for transfers between devices, body(): attended_full = lax.all_gather(attended, 'wid', axis=1, tiled=True)  36.1 us
    all_gather x1, waiting for transfers between devices, body(): key_values = lax.all_gather(qkv[:, 1:3], 'tok', axis=0, tiled=True)  31.9 us
    all_gather x1, blocking collectives, body(): shift_scale = lax.all_gather(modulation[:2], 'wid', axis=1, tiled=True)  23.7 us
    all_gather x1, waiting for transfers between devices, body(): residual_full = lax.all_gather(residual_in, 'wid', axis=1, tiled=True)  20.4 us
    all_to_all x1, waiting for transfers between devices, body(): lax.all_to_all(w_out, 'wid', split_axis=1, concat_axis=0, tiled=True)  17.5 us
    dot_general x1, matrix products, body(): jnp.dot(queries, key_part.T, preferred_element_type=jnp.float32)  14.7 us
    reduce_sum x1, other arithmetic, body(): row_sum = jnp.sum(shifted, axis=1, keepdims=True)  14.3 us
    dot_general x1, matrix products, body(): jnp.dot(shifted.astype(jnp.bfloat16), value_part, preferred_element_type=...  14.2 us
  transfers between devices with their start and end apart: 11, of which 6 were waited for; matrix products, arithmetic and copies ran while one was open for 10% of the time, Pallas kernels for 0%

profile of v1, /device:TPU:0, one launch (start us, length us, event | category | flops | bytes accessed | tf_op | source)
XLA Modules:
  0.0 245.3 jit_solution(8006778684488986825)
XLA Ops:
  6.5 0.7 convert_element_type.47
  7.3 0.7 convert_element_type.48
  7.9 1.9 add_convert_fusion.1
  9.8 0.0 all-gather.5.cloned.1.call-update
  9.9 0.0 all-gather.7.cloned.1.call-start
  9.9 3.6 %collective-permute-start = (bf16[384,3,128]{2,0,1:T(8,128)(2,1)}, bf16[384,3,128]{2,0,1:T(8,128)(2,1)S(1)}, u32[]{:S(2)}, u32[]{:S(2)}) collective-permute-start(bf16[384,3,128]{2,0,1:T(8,128)(2,1)} %param.12), channel_id=1, source_target_pairs={{0,112},{16,0},{32,16},{48,32},{64,48},{80,64},{96,80},{112,96},{1... | collective-permute-start | bytes 884744 | tf_op jit(solution)/shard_map/ppermute | solution.py:22
  13.5 0.0 collective-permute-start.1
  14.2 0.4 fusion.55
  14.6 23.7 %all-gather = bf16[16,192,2]{1,2,0:T(2,128)(2,1)S(1)} all-gather(bf16[1,192,2]{1,2,0:T(2,128)(2,1)S(1)} %slice_bitcast_fusion.10), channel_id=1, replica_groups=mesh['tok'=8,'wid'=16] {'wid'}, dimensions={0}, use_global_device_ids=true | all-gather | bytes 13056 | tf_op jit(solution)/shard_map/all_gather | solution.py:53
  38.3 0.1 reshape.28
  38.4 0.0 collective-permute-done.1
  38.4 0.0 collective-permute-start.3
  38.5 3.0 %collective-permute-start.2 = (bf16[384,3,128]{2,0,1:T(8,128)(2,1)S(1)}, bf16[384,3,128]{2,0,1:T(8,128)(2,1)S(1)}, u32[]{:S(2)}, u32[]{:S(2)}) collective-permute-start(bf16[384,3,128]{2,0,1:T(8,128)(2,1)S(1)} %collective-permute-done), channel_id=1, source_target_pairs={{0,112},{16,0},{32,16},{48,32},{64,48},{80,64},{96,80},{112,96},{1... | collective-permute-start | bytes 884744 | tf_op jit(solution)/shard_map/ppermute | solution.py:22
  41.5 4.4 %collective-permute-done.3 = bf16[384,3,128]{2,0,1:T(8,128)(2,1)S(1)} collective-permute-done((bf16[384,3,128]{2,0,1:T(8,128)(2,1)S(1)}, bf16[384,3,128]{2,0,1:T(8,128)(2,1)S(1)}, u32[]{:S(2)}, u32[]{:S(2)}) %collective-permute-start.3) | collective-permute-done | bytes 294944 | tf_op jit(solution)/shard_map/ppermute | solution.py:20
  46.0 3.0 %collective-permute-start.4 = (bf16[384,3,128]{2,0,1:T(8,128)(2,1)S(1)}, bf16[384,3,128]{2,0,1:T(8,128)(2,1)S(1)}, u32[]{:S(2)}, u32[]{:S(2)}) collective-permute-start(bf16[384,3,128]{2,0,1:T(8,128)(2,1)S(1)} %collective-permute-done.2), channel_id=1, source_target_pairs={{0,112},{16,0},{32,16},{48,32},{64,48},{80,64},{96,80},{112,96},{1... | collective-permute-start | bytes 884744 | tf_op jit(solution)/shard_map/ppermute | solution.py:22
  48.9 4.2 %collective-permute-done.5 = bf16[384,3,128]{2,0,1:T(8,128)(2,1)S(1)} collective-permute-done((bf16[384,3,128]{2,0,1:T(8,128)(2,1)S(1)}, bf16[384,3,128]{2,0,1:T(8,128)(2,1)S(1)}, u32[]{:S(2)}, u32[]{:S(2)}) %collective-permute-start.5) | collective-permute-done | bytes 294944 | tf_op jit(solution)/shard_map/ppermute | solution.py:20
  53.2 0.0 collective-permute-start.6
  53.2 20.4 %all-gather.5.cloned.1.call-done = bf16[1024,3072]{0,1:T(8,128)(2,1)} async-done(((bf16[1024,192]{0,1:T(8,128)(2,1)}), bf16[1024,3072]{0,1:T(8,128)(2,1)}) %all-gather.5.cloned.1.call-update) | async-done | bytes 6291472 | tf_op jit(solution)/shard_map/all_gather | solution.py:42
  73.6 8.6 %copy.22 = bf16[1024,3072]{1,0:T(8,128)(2,1)} copy(bf16[1024,3072]{0,1:T(8,128)(2,1)} %all-gather.5.cloned.1.call-done) | data formatting | bytes 12582912 | tf_op jit(solution)/shard_map/all_gather | solution.py:42
  82.3 4.8 %convert_reduce_fusion = (f32[1024]{0:T(1024)S(1)}, f32[1024]{0:T(1024)S(1)}) fusion(bf16[1024,3072]{1,0:T(8,128)(2,1)} %copy.22), kind=kLoop, calls=%fused_computation.6 | loop fusion | flops 12580864 | bytes 6299648 | tf_op jit(solution)/shard_map/reduce_sum | solution.py:55
  87.1 0.0 copy-start.6
  87.1 3.8 %fusion.7 = bf16[1024,3072]{1,0:T(8,128)(2,1)S(1)} fusion(bf16[1024,3072]{1,0:T(8,128)(2,1)S(1)} %copy-done.2, f32[3072]{0:T(1024)S(1)} %bitcast.79, f32[3072]{0:T(1024)S(1)} %bitcast.78, f32[1024]{0:T(1024)S(1)} %get-tuple-element.8, f32[1024]{0:T(1024)S(1)} %get-tuple-element.7), kind=kLoop, calls=%fused_computation.11 | loop fusion | flops 18874368 | bytes 12615680 | tf_op jit(solution)/shard_map/convert_element_type | solution.py:30
  90.9 0.6 fusion.33
  91.6 0.6 fusion.25
  92.2 0.6 fusion.27
  92.8 0.6 fusion.29
  93.5 0.6 fusion.31
  94.1 0.6 fusion.21
  94.8 0.0 collective-permute-done.4
  94.8 0.6 fusion.23
  95.4 0.0 collective-permute-done.6
  95.4 1.0 add_convert_fusion
  96.5 0.8 slice.37
  97.3 0.0 all-gather.7.cloned.1.call-update
  97.3 0.2 all-gather.9.cloned.1.call-start
  97.6 31.9 %all-gather.7.cloned.1.call-done = bf16[8192,2,128]{2,0,1:T(8,128)(2,1)} async-done(((bf16[1024,2,128]{2,0,1:T(8,128)(2,1)}), bf16[8192,2,128]{2,0,1:T(8,128)(2,1)}) %all-gather.7.cloned.1.call-update) | async-done | bytes 4194320 | tf_op jit(solution)/shard_map/all_gather | solution.py:72
  129.4 14.7 %multiply_reduce_fusion = (f32[1024]{0:T(1024)S(1)}, f32[1024,8192]{1,0:T(8,128)}) fusion(bf16[8192,2,128]{2,0,1:T(8,128)(2,1)} %all-gather.7.cloned.1.call-done, bf16[1024,3,128]{2,0,1:T(8,128)(2,1)S(1)} %add_convert_fusion), kind=kOutput, calls=%fused_computation.1 | convolution fusion | flops 2164259840 | bytes 35917824 | tf_op jit(solution)/shard_map/dot_general | solution.py:76
  144.1 14.3 %fusion = f32[1024]{0:T(1024)S(1)} fusion(f32[1024,8192]{1,0:T(8,128)} %get-tuple-element.10, f32[1024]{0:T(1024)S(1)} %get-tuple-element.9), kind=kLoop, calls=%fused_computation.2 | loop fusion | flops 25164800 | bytes 33562624 | tf_op jit(solution)/shard_map/reduce_sum | solution.py:78
  158.4 0.0 copy-start.5
  158.4 0.0 copy-start.3
  158.4 0.0 copy-start.1
  158.4 14.2 %fusion.15 = bf16[1024,128]{1,0:T(8,128)(2,1)} fusion(bf16[8192,2,128]{2,0,1:T(8,128)(2,1)S(1)} %copy-done.4, f32[1024,8192]{1,0:T(8,128)} %get-tuple-element.10, f32[1024]{0:T(1024)S(1)} %get-tuple-element.9, f32[1024]{0:T(1024)S(1)} %fusion), kind=kOutput, calls=%fused_computation.21 | convolution fusion | flops 2172911616 | bytes 35921920 | tf_op jit(solution)/shard_map/dot_general | solution.py:79
  172.6 0.0 all-gather.9.cloned.1.call-update
  172.6 1.2 copy.24
  173.8 6.8 %all-to-all-start = ((bf16[128,16,192]{0,2,1:T(8,128)(2,1)}), bf16[128,16,192]{0,2,1:T(8,128)(2,1)S(1)}, u32[]{:S(2)}, u32[]{:S(2)}) async-start(bf16[128,16,192]{0,2,1:T(8,128)(2,1)} %bitcast.20), calls=%async_computation | async-start | bytes 1572864 | tf_op jit(solution)/shard_map/all_to_all | solution.py:41
  180.6 17.5 %all-to-all-done = bf16[128,16,192]{0,2,1:T(8,128)(2,1)S(1)} async-done(((bf16[128,16,192]{0,2,1:T(8,128)(2,1)}), bf16[128,16,192]{0,2,1:T(8,128)(2,1)S(1)}, u32[]{:S(2)}, u32[]{:S(2)}) %all-to-all-start) | async-done | bytes 786464 | tf_op jit(solution)/shard_map/all_to_all | solution.py:41
  198.2 36.1 %all-gather.9.cloned.1.call-done = bf16[1024,2048]{1,0:T(8,128)(2,1)} async-done(((bf16[1024,128]{1,0:T(8,128)(2,1)}), bf16[1024,2048]{1,0:T(8,128)(2,1)}) %all-gather.9.cloned.1.call-update) | async-done | bytes 4194320 | tf_op jit(solution)/shard_map/all_gather | solution.py:81
  234.3 4.5 %fusion.11 = bf16[1024,192]{0,1:T(8,128)(2,1)} fusion(bf16[1024,2048]{1,0:T(8,128)(2,1)} %all-gather.9.cloned.1.call-done, bf16[1024,192]{0,1:T(8,128)(2,1)S(1)} %copy-done.3, f32[192]{0:T(256)S(1)} %bitcast.83, bf16[128,16,192]{0,2,1:T(8,128)(2,1)S(1)} %all-to-all-done), kind=kOutput, calls=%fused_computation.19 | convolution fusion | flops 806092800 | bytes 5767936 | tf_op jit(solution)/shard_map/dot_general | solution.py:82
  (23 shorter events, 0.2 us)
Async XLA Ops:
  6.5 7.7 %copy-start = (bf16[256,3,192]{0,2,1:T(8,128)(2,1)S(1)}, bf16[256,3,192]{0,2,1:T(8,128)(2,1)}, u32[]{:S(2)}) copy-start(bf16[256,3,192]{0,2,1:T(8,128)(2,1)} %param.11) | copy-start | bytes 884740
  6.5 67.1 %all-gather.5.cloned.1.call-start = ((), (), s32[]{:S(2)}) async-start(), calls=%async_computation.1 | async-start | bytes 6684672 | tf_op jit(solution)/shard_map/all_gather | solution.py:42
  9.9 119.6 %all-gather.7.cloned.1.call-start = ((), (), s32[]{:S(2)}) async-start(), calls=%async_computation.2 | async-start | bytes 4718592 | tf_op jit(solution)/shard_map/all_gather | solution.py:72
  9.9 28.6 %collective-permute-start = (bf16[384,3,128]{2,0,1:T(8,128)(2,1)}, bf16[384,3,128]{2,0,1:T(8,128)(2,1)S(1)}, u32[]{:S(2)}, u32[]{:S(2)}) collective-permute-start(bf16[384,3,128]{2,0,1:T(8,128)(2,1)} %param.12), channel_id=1, source_target_pairs={{0,112},{16,0},{32,16},{48,32},{64,48},{80,64},{96,80},{112,96},{1... | collective-permute-start | bytes 884744 | tf_op jit(solution)/shard_map/ppermute | solution.py:22
  13.5 24.9 %collective-permute-start.1 = (bf16[384,3,128]{2,0,1:T(8,128)(2,1)}, bf16[384,3,128]{2,0,1:T(8,128)(2,1)S(1)}, u32[]{:S(2)}, u32[]{:S(2)}) collective-permute-start(bf16[384,3,128]{2,0,1:T(8,128)(2,1)} %param.12), channel_id=1, source_target_pairs={{0,16},{16,32},{32,48},{48,64},{64,80},{80,96},{96,112},{112,0},{1... | collective-permute-start | bytes 884744 | tf_op jit(solution)/shard_map/ppermute | solution.py:20
  38.4 7.4 %collective-permute-start.3 = (bf16[384,3,128]{2,0,1:T(8,128)(2,1)S(1)}, bf16[384,3,128]{2,0,1:T(8,128)(2,1)S(1)}, u32[]{:S(2)}, u32[]{:S(2)}) collective-permute-start(bf16[384,3,128]{2,0,1:T(8,128)(2,1)S(1)} %collective-permute-done.1), channel_id=1, source_target_pairs={{0,16},{16,32},{32,48},{48,64},{64,80},{80,96},{96,112},{112,0},{1... | collective-permute-start | bytes 884744 | tf_op jit(solution)/shard_map/ppermute | solution.py:20
  38.5 7.5 %collective-permute-start.2 = (bf16[384,3,128]{2,0,1:T(8,128)(2,1)S(1)}, bf16[384,3,128]{2,0,1:T(8,128)(2,1)S(1)}, u32[]{:S(2)}, u32[]{:S(2)}) collective-permute-start(bf16[384,3,128]{2,0,1:T(8,128)(2,1)S(1)} %collective-permute-done), channel_id=1, source_target_pairs={{0,112},{16,0},{32,16},{48,32},{64,48},{80,64},{96,80},{112,96},{1... | collective-permute-start | bytes 884744 | tf_op jit(solution)/shard_map/ppermute | solution.py:22
  45.8 7.4 %collective-permute-start.5 = (bf16[384,3,128]{2,0,1:T(8,128)(2,1)S(1)}, bf16[384,3,128]{2,0,1:T(8,128)(2,1)S(1)}, u32[]{:S(2)}, u32[]{:S(2)}) collective-permute-start(bf16[384,3,128]{2,0,1:T(8,128)(2,1)S(1)} %collective-permute-done.3), channel_id=1, source_target_pairs={{0,16},{16,32},{32,48},{48,64},{64,80},{80,96},{96,112},{112,0},{1... | collective-permute-start | bytes 884744 | tf_op jit(solution)/shard_map/ppermute | solution.py:20
  46.0 48.8 %collective-permute-start.4 = (bf16[384,3,128]{2,0,1:T(8,128)(2,1)S(1)}, bf16[384,3,128]{2,0,1:T(8,128)(2,1)S(1)}, u32[]{:S(2)}, u32[]{:S(2)}) collective-permute-start(bf16[384,3,128]{2,0,1:T(8,128)(2,1)S(1)} %collective-permute-done.2), channel_id=1, source_target_pairs={{0,112},{16,0},{32,16},{48,32},{64,48},{80,64},{96,80},{112,96},{1... | collective-permute-start | bytes 884744 | tf_op jit(solution)/shard_map/ppermute | solution.py:22
  53.2 42.2 %collective-permute-start.6 = (bf16[384,3,128]{2,0,1:T(8,128)(2,1)S(1)}, bf16[384,3,128]{2,0,1:T(8,128)(2,1)S(1)}, u32[]{:S(2)}, u32[]{:S(2)}) collective-permute-start(bf16[384,3,128]{2,0,1:T(8,128)(2,1)S(1)} %collective-permute-done.5), channel_id=1, source_target_pairs={{0,16},{16,32},{32,48},{48,64},{64,80},{80,96},{96,112},{112,0},{1... | collective-permute-start | bytes 884744 | tf_op jit(solution)/shard_map/ppermute | solution.py:20
  82.3 4.8 %copy-start.2 = (bf16[1024,3072]{1,0:T(8,128)(2,1)S(1)}, bf16[1024,3072]{1,0:T(8,128)(2,1)}, u32[]{:S(2)}) copy-start(bf16[1024,3072]{1,0:T(8,128)(2,1)} %copy.22) | copy-start | bytes 18874372
  87.1 3.8 %copy-start.6 = (bf16[384,3,128]{2,0,1:T(8,128)(2,1)S(1)}, bf16[384,3,128]{2,0,1:T(8,128)(2,1)}, u32[]{:S(2)}) copy-start(bf16[384,3,128]{2,0,1:T(8,128)(2,1)} %param.12) | copy-start | bytes 884740
  97.3 136.9 %all-gather.9.cloned.1.call-start = ((), (), s32[]{:S(2)}) async-start(), calls=%async_computation.3 | async-start | bytes 4456448 | tf_op jit(solution)/shard_map/all_gather | solution.py:81
  144.1 14.3 %copy-start.4 = (bf16[8192,2,128]{2,0,1:T(8,128)(2,1)S(1)}, bf16[8192,2,128]{2,0,1:T(8,128)(2,1)}, u32[]{:S(2)}) copy-start(bf16[8192,2,128]{2,0,1:T(8,128)(2,1)} %all-gather.7.cloned.1.call-done) | copy-start | bytes 12582916
  158.4 14.2 %copy-start.5 = (bf16[128,3072]{1,0:T(8,128)(2,1)S(1)}, bf16[128,3072]{1,0:T(8,128)(2,1)}, u32[]{:S(2)}) copy-start(bf16[128,3072]{1,0:T(8,128)(2,1)} %param.13) | copy-start | bytes 2359300
  158.4 75.8 %copy-start.3 = (bf16[1024,192]{0,1:T(8,128)(2,1)S(1)}, bf16[1024,192]{0,1:T(8,128)(2,1)}, u32[]{:S(2)}) copy-start(bf16[1024,192]{0,1:T(8,128)(2,1)} %add_convert_fusion.1) | copy-start | bytes 1179652
  158.4 80.3 %copy-start.1 = (bf16[256,3,192]{0,2,1:T(8,128)(2,1)S(1)}, bf16[256,3,192]{0,2,1:T(8,128)(2,1)}, u32[]{:S(2)}) copy-start(bf16[256,3,192]{0,2,1:T(8,128)(2,1)} %param.11) | copy-start | bytes 884740
  173.8 24.4 %all-to-all-start = ((bf16[128,16,192]{0,2,1:T(8,128)(2,1)}), bf16[128,16,192]{0,2,1:T(8,128)(2,1)S(1)}, u32[]{:S(2)}, u32[]{:S(2)}) async-start(bf16[128,16,192]{0,2,1:T(8,128)(2,1)} %bitcast.20), calls=%async_computation | async-start | bytes 1572864 | tf_op jit(solution)/shard_map/all_to_all | solution.py:41
Sparse Core Ops, SparseCore 0:
  10.0 63.5 all-gather.4
  97.4 31.9 all-gather.6
  172.8 61.4 all-gather.8
